TPU v7x, 32 devices: a whole 2x2x4 slice. The times are simulated.
32 devices in a mesh: row: 4 (over y, core), col: 8 (over z, x).
Axes of the slice: x: 2, y: 2, z: 4, core: 2. Of those that a mesh axis runs over, the one named last changes fastest.
Arguments:
- node_feats: bfloat16 [8192, 256], P(('row', 'col')), may hold values from -6 to 6
- weight: bfloat16 [256, 256], replicated, may hold values from -0.375 to 0.375
- cotangent: bfloat16 [8192, 256], P(('row', 'col')), may hold values from -6 to 6
- band_tiles: bfloat16 [384, 128, 128], P(('row', 'col')), may hold values from 0 to 0.049804688
- band_coords: int32 [384, 2], P(('row', 'col')), may hold values from 0 to 5, as said below
- bound_tiles: bfloat16 [1280, 128, 128], P(('row', 'col')), may hold values from 0 to 0.049804688
- bound_coords: int32 [1280, 2], P(('row', 'col')), may hold values from 0 to 7, as said below
- bound_count: int32 [32], P(('row', 'col')), may hold values from 0 to 40, as said below
- recv_lists: int32 [32, 8], P(('row', 'col')), may hold values from -1 to 1, as said below
- send_lists: int32 [32, 8], P(('row', 'col')), may hold values from -1 to 1, as said below
- reorder: int32 [32, 256], P(('row', 'col')), may hold values from 0 to 255, each once within a row
Outputs:
- node_out: bfloat16 [8192, 256], P(('row', 'col'))
- feat_grad: bfloat16 [8192, 256], P(('row', 'col'))
- weight_grad: float32 [256, 256], replicated
Inputs may be any that keep to these rules, and one draw needn't show every extreme that they name: recv_lists[r * 8 + c, s] is a row block of device r * 8 + s, below 2, or -1 for none; it is -1 where s = c. In every row group one device receives a block from every other column. send_lists[r * 8 + s, c] equals recv_lists[r * 8 + c, s]. bound_count[d] is at least the number of entries of recv_lists[d] that are not -1; in every row group one device has all 40 slots live. `bound_coords`: pairs (row block below 2, owner column below 8); for k < bound_count[d] the owner column s of slot k has recv_lists[d, s] >= 0, and every such column is named by one of them; slots from bound_count[d] on are not used. `band_coords`: pairs (row block below 2, extended column block below (768) / 128); no pair twice on one device. `reorder`: each row is a permutation.
All inputs are finite; a program needn't handle non-finite values.
Results may differ from a plain program's by a relative error of at most 0.0095.
Values may be sent and summed in bfloat16 or wider, within the bound.
No kernel may reach another device: no remote copies, remote signals or barrier semaphores. Data moves between devices by JAX's collectives and lax.ppermute only.
A program may use at most 64 MiB of HBM per device.

v0:
```python
import jax
import jax.numpy as jnp
from jax import lax
from jax.sharding import PartitionSpec as P

BW = 256


def padded_2(cells, sides, width):
    for axis, dim in sides:
        count = lax.axis_size(axis)
        head = lax.slice_in_dim(cells, 0, width, axis=dim)
        tail = lax.slice_in_dim(cells, cells.shape[dim] - width, cells.shape[dim], axis=dim)
        cells = jnp.concatenate(
            [
                lax.ppermute(tail, axis, [(i, (i + 1) % count) for i in range(count)]),
                cells,
                lax.ppermute(head, axis, [((i + 1) % count, i) for i in range(count)]),
            ],
            axis=dim,
        )
    return cells


def split_sum(selector, terms):
    high_part = terms.astype(jnp.bfloat16)
    low_part = (terms - high_part.astype(jnp.float32)).astype(jnp.bfloat16)
    pick = selector.astype(jnp.bfloat16)
    upper_sum = jnp.einsum("rk,kaf->raf", pick, high_part, preferred_element_type=jnp.float32)
    lower_sum = jnp.einsum("rk,kaf->raf", pick, low_part, preferred_element_type=jnp.float32)
    return upper_sum + lower_sum


def on_device(
    node_feats,
    weight,
    cotangent,
    band_tiles,
    band_coords,
    bound_tiles,
    bound_coords,
    bound_count,
    recv_lists,
    send_lists,
    reorder,
):
    tile_size = band_tiles.shape[1]
    row_count = node_feats.shape[0]
    width_feat = node_feats.shape[1]
    tile_rows = row_count // tile_size
    rim_tiles = BW // tile_size
    col_tiles = tile_rows + 2 * rim_tiles
    ext_count = row_count + 2 * BW
    peers = lax.axis_size("col")
    slot_total = bound_tiles.shape[0]
    order = reorder[0]
    inverse = (
        jnp.zeros((row_count,), jnp.int32).at[order].set(jnp.arange(row_count, dtype=jnp.int32))
    )
    x_band = jnp.take(node_feats, order, axis=0)
    hidden = jnp.dot(x_band, weight, preferred_element_type=jnp.float32).astype(jnp.bfloat16)
    band_row_ids = band_coords[:, 0]
    band_col_ids = band_coords[:, 1]
    band_dense = jnp.zeros((tile_rows, tile_size, col_tiles, tile_size), jnp.bfloat16)
    band_dense = (
        band_dense.at[band_row_ids, :, band_col_ids].set(band_tiles).reshape(row_count, ext_count)
    )
    extended = padded_2(hidden, (("row", 0),), BW)
    mixed = jnp.dot(band_dense, extended, preferred_element_type=jnp.float32)
    blocks = hidden.reshape(tile_rows, tile_size, width_feat)
    giving = send_lists[0]
    outgoing = jnp.where(
        (giving >= 0)[:, None, None],
        jnp.take(blocks, jnp.maximum(giving, 0), axis=0),
        jnp.zeros((), jnp.bfloat16),
    )
    arrived = lax.all_to_all(outgoing, "col", split_axis=0, concat_axis=0, tiled=True)
    tile_range = jnp.arange(tile_rows, dtype=jnp.int32)
    live_slots = jnp.arange(slot_total, dtype=jnp.int32) < bound_count[0]
    bound_row_ids = bound_coords[:, 0]
    bound_owner = bound_coords[:, 1]
    bound_onehot = (bound_row_ids[None, :] == tile_range[:, None]) & live_slots[None, :]
    slot_rows = jnp.take(arrived, bound_owner, axis=0).reshape(slot_total * tile_size, width_feat)
    placed = jnp.einsum(
        "rk,kab->rakb",
        bound_onehot.astype(jnp.bfloat16),
        bound_tiles,
        preferred_element_type=jnp.bfloat16,
    )
    placed = placed.reshape(row_count, slot_total * tile_size)
    mixed = mixed + jnp.dot(placed, slot_rows, preferred_element_type=jnp.float32)
    out_band = jax.nn.silu(mixed).astype(jnp.bfloat16)
    node_out = jnp.take(out_band, inverse, axis=0)
    grad_band = jnp.take(cotangent, order, axis=0).astype(jnp.float32)
    sigma = jax.nn.sigmoid(mixed)
    slope = (grad_band * sigma * (1.0 + mixed * (1.0 - sigma))).astype(jnp.bfloat16)
    slope_blocks = slope.reshape(tile_rows, tile_size, width_feat)
    ext_grad = lax.dot_general(
        band_dense, slope, (((0,), (0,)), ((), ())), preferred_element_type=jnp.float32
    )
    rim_terms = jnp.concatenate([ext_grad[:BW], ext_grad[BW + row_count :]], axis=0).astype(
        jnp.bfloat16
    )
    padded = padded_2(rim_terms, (("row", 0),), BW)
    grad_hidden = ext_grad[BW : BW + row_count]
    grad_hidden = grad_hidden.at[:BW].add(padded[:BW].astype(jnp.float32))
    grad_hidden = grad_hidden.at[row_count - BW :].add(padded[3 * BW :].astype(jnp.float32))
    slot_back = jnp.einsum(
        "kab,kaf->kbf",
        bound_tiles,
        jnp.take(slope_blocks, bound_row_ids, axis=0),
        preferred_element_type=jnp.float32,
    )
    owner_range = jnp.arange(peers, dtype=jnp.int32)
    owner_onehot = (bound_owner[None, :] == owner_range[:, None]) & live_slots[None, :]
    to_owner = split_sum(owner_onehot, slot_back).astype(jnp.bfloat16)
    returned = lax.all_to_all(to_owner, "col", split_axis=0, concat_axis=0, tiled=True)
    block_onehot = (giving[None, :] == tile_range[:, None]).astype(jnp.bfloat16)
    from_peers = jnp.einsum(
        "bs,saf->baf", block_onehot, returned, preferred_element_type=jnp.float32
    )
    grad_hidden = grad_hidden + from_peers.reshape(row_count, width_feat)
    grad_round = grad_hidden.astype(jnp.bfloat16)
    partial_weight = lax.dot_general(
        x_band, grad_round, (((0,), (0,)), ((), ())), preferred_element_type=jnp.float32
    )
    nodes_all = row_count * lax.axis_size("row") * peers
    weight_grad = lax.psum(partial_weight, ("row", "col")) * nodes_all ** (-0.5)
    feat_band = lax.dot_general(
        grad_round, weight, (((1,), (1,)), ((), ())), preferred_element_type=jnp.float32
    ).astype(jnp.bfloat16)
    feat_grad = jnp.take(feat_band, inverse, axis=0)
    return (node_out, feat_grad, weight_grad)


def solution(mesh):
    in_specs = (
        P(("row", "col"), None),
        P(),
        P(("row", "col"), None),
        P(("row", "col"), None, None),
        P(("row", "col"), None),
        P(("row", "col"), None, None),
        P(("row", "col"), None),
        P(("row", "col")),
        P(("row", "col"), None),
        P(("row", "col"), None),
        P(("row", "col"), None),
    )
    out_specs = (P(("row", "col"), None), P(("row", "col"), None), P())
    return jax.shard_map(
        on_device, mesh=mesh, in_specs=in_specs, out_specs=out_specs, check_vma=False
    )
```

profile of v0, /device:TPU:0, one launch (start us, length us, event | category | flops | bytes accessed | tf_op | source)
XLA Modules:
  0.0 214.7 jit_solution(14946147041477789685)
XLA Ops:
  8.7 1.9 gather_fusion.3
  11.4 2.0 collective-permute-start.1
  16.3 6.5 %all-to-all-start = ((bf16[8,128,256]{2,1,0:T(8,128)(2,1)}), bf16[8,128,256]{2,1,0:T(8,128)(2,1)S(1)}, u32[]{:S(2)}, u32[]{:S(2)}) async-start(bf16[8,128,256]{2,1,0:T(8,128)(2,1)} %select_select_fusion), calls=%async_computation | async-start | bytes 1048576 | tf_op jit(solution)/shard_map/all_to_all | solution.py:77
  26.1 1.8 gather_fusion.5
  28.0 2.0 scatter_fusion
  30.1 1.1 copy.19
  31.2 2.1 scatter_custom_fusion.1
  33.8 1.7 broadcast_multiply_fusion
  35.6 1.8 all-to-all-done
  38.4 1.4 copy-done.4
  40.8 1.3 multiply_convert_fusion
  42.2 2.4 %gather_fusion.2 = bf16[40,128,256]{2,1,0:T(8,128)(2,1)} fusion(bf16[2,128,256]{2,1,0:T(8,128)(2,1)S(1)} %bitcast.73, s32[1024]{0:T(1024)S(1)} %pad_clamp_fusion), kind=kCustom, calls=%fused_computation.6 | custom fusion | bytes 5243040 | tf_op jit(solution)/shard_map/jit(_take)/gather | solution.py:111
  44.6 4.9 %fusion = (bf16[40,128,256]{1,2,0:T(8,128)(2,1)S(1)}, bf16[40,128,256]{1,2,0:T(8,128)(2,1)}) fusion(bf16[40,128,128]{2,1,0:T(8,128)(2,1)} %param.26, bf16[40,128,256]{2,1,0:T(8,128)(2,1)} %gather_fusion.2, pred[40]{0:T(512)(128)(4,1)S(1)} %copy-done.16), kind=kOutput, calls=%fused_computation.11 | convolution fusion | flops 342097920 | bytes 9175080 | tf_op jit(solution)/shard_map/kab,kaf->kbf/dot_general | solution.py:108
  49.5 4.7 %copy.22 = bf16[40,128,256]{2,0,1:T(8,128)(2,1)} copy(bf16[40,128,256]{1,2,0:T(8,128)(2,1)} %get-tuple-element.45) | data formatting | bytes 5242880 | tf_op jit(solution)/shard_map/convert_element_type | solution.py:26
  54.2 3.4 %copy.23 = bf16[40,128,256]{2,0,1:T(8,128)(2,1)} copy(bf16[40,128,256]{1,2,0:T(8,128)(2,1)S(1)} %get-tuple-element.44) | data formatting | bytes 5242880 | tf_op jit(solution)/shard_map/convert_element_type | solution.py:27
  57.6 2.5 %fusion.28 = f32[8,128,256]{2,0,1:T(8,128)S(1)} fusion(bf16[40,128,256]{2,0,1:T(8,128)(2,1)} %copy.22, s32[40]{0:T(128)S(1)} %get-tuple-element.50, pred[40]{0:T(512)(128)(4,1)S(1)} %copy-done.15), kind=kOutput, calls=%fused_computation.62 | convolution fusion | flops 20972160 | bytes 3670216 | tf_op jit(solution)/shard_map/rk,kaf->raf/dot_general | solution.py:29
  61.6 4.2 %all-to-all-start.1 = ((bf16[8,128,256]{2,1,0:T(8,128)(2,1)}), bf16[8,128,256]{2,1,0:T(8,128)(2,1)S(1)}, u32[]{:S(2)}, u32[]{:S(2)}) async-start(bf16[8,128,256]{2,1,0:T(8,128)(2,1)} %copy.24), calls=%async_computation.1 | async-start | bytes 1048576 | tf_op jit(solution)/shard_map/all_to_all | solution.py:117
  66.3 1.7 collective-permute-start.3
  68.0 1.1 gather_fusion.4
  69.2 10.8 %all-to-all-done.1 = bf16[8,128,256]{2,1,0:T(8,128)(2,1)S(1)} async-done(((bf16[8,128,256]{2,1,0:T(8,128)(2,1)}), bf16[8,128,256]{2,1,0:T(8,128)(2,1)S(1)}, u32[]{:S(2)}, u32[]{:S(2)}) %all-to-all-start.1) | async-done | bytes 524320 | tf_op jit(solution)/shard_map/all_to_all | solution.py:117
  80.7 1.0 fusion.24
  81.7 1.1 gather_fusion.6
  83.7 122.5 %all-reduce.2.cloned.1.call-done = f32[256,256]{1,0:T(8,128)} async-done(((f32[256,256]{1,0:T(8,128)}), f32[256,256]{1,0:T(8,128)}) %all-reduce.2.cloned.1.call-update) | async-done | bytes 262160 | tf_op jit(solution)/shard_map/psum | solution.py:128
  206.1 1.7 broadcast_multiply_fusion.1
  (86 shorter events, 13.8 us)
Async XLA Ops:
  7.2 3.4 %copy-start = (bf16[256,256]{1,0:T(8,128)(2,1)S(1)}, bf16[256,256]{1,0:T(8,128)(2,1)}, u32[]{:S(2)}) copy-start(bf16[256,256]{1,0:T(8,128)(2,1)} %param.22) | copy-start | bytes 393220
  7.2 15.6 %copy-start.11 = (s32[1,256]{1,0:T(1,128)S(1)}, s32[1,256]{1,0:T(1,128)}, u32[]{:S(2)}) copy-start(s32[1,256]{1,0:T(1,128)} %param.30) | copy-start | bytes 3076
  7.2 16.2 %copy-start.9 = (s32[40,2]{0,1:T(2,128)S(1)}, s32[40,2]{0,1:T(2,128)}, u32[]{:S(2)}) copy-start(s32[40,2]{0,1:T(2,128)} %param.27) | copy-start | bytes 964
  7.2 17.4 %copy-start.21 = (s32[12,2]{0,1:T(2,128)S(1)}, s32[12,2]{0,1:T(2,128)}, u32[]{:S(2)}) copy-start(s32[12,2]{0,1:T(2,128)} %param.25) | copy-start | bytes 292
  7.2 18.0 %copy-start.3 = (bf16[40,128,128]{2,1,0:T(8,128)(2,1)S(1)}, bf16[40,128,128]{2,1,0:T(8,128)(2,1)}, u32[]{:S(2)}) copy-start(bf16[40,128,128]{2,1,0:T(8,128)(2,1)} %param.26) | copy-start | bytes 3932164
  8.7 5.3 %copy-start.12 = (pred[256]{0:T(512)(128)(4,1)}, pred[256]{0:T(512)(128)(4,1)S(1)}, u32[]{:S(2)}) copy-start(pred[256]{0:T(512)(128)(4,1)S(1)} %compare_and_fusion.1) | copy-start | bytes 772
  10.6 4.1 %copy-start.6 = (bf16[256,256]{1,0:T(8,128)(2,1)}, bf16[256,256]{1,0:T(8,128)(2,1)S(1)}, u32[]{:S(2)}) copy-start(bf16[256,256]{1,0:T(8,128)(2,1)S(1)} %gather_fusion.3) | copy-start | bytes 393220
  10.9 29.8 %collective-permute-start = (bf16[256,256]{1,0:T(8,128)(2,1)S(1)}, bf16[256,256]{1,0:T(8,128)(2,1)}, u32[]{:S(2)}, u32[]{:S(2)}) collective-permute-start(bf16[256,256]{1,0:T(8,128)(2,1)S(1)} %convolution_convert_fusion.1), channel_id=1, source_target_pairs={{0,8},{8,16},{16,24},{24,0},{1,9},{9,17},{17,25},{25,1},{2,10},{10... | collective-permute-start | bytes 393224 | tf_op jit(solution)/shard_map/ppermute | solution.py:16
  11.4 29.3 %collective-permute-start.1 = (bf16[256,256]{1,0:T(8,128)(2,1)S(1)}, bf16[256,256]{1,0:T(8,128)(2,1)}, u32[]{:S(2)}, u32[]{:S(2)}) collective-permute-start(bf16[256,256]{1,0:T(8,128)(2,1)S(1)} %convolution_convert_fusion.1), channel_id=1, source_target_pairs={{8,0},{16,8},{24,16},{0,24},{9,1},{17,9},{25,17},{1,25},{10,2},{18... | collective-permute-start | bytes 393224 | tf_op jit(solution)/shard_map/ppermute | solution.py:18
  15.3 10.8 %copy-start.2 = (bf16[256,256]{1,0:T(8,128)(2,1)S(1)}, bf16[256,256]{1,0:T(8,128)(2,1)}, u32[]{:S(2)}) copy-start(bf16[256,256]{1,0:T(8,128)(2,1)} %param.23) | copy-start | bytes 393220
  16.3 21.1 %all-to-all-start = ((bf16[8,128,256]{2,1,0:T(8,128)(2,1)}), bf16[8,128,256]{2,1,0:T(8,128)(2,1)S(1)}, u32[]{:S(2)}, u32[]{:S(2)}) async-start(bf16[8,128,256]{2,1,0:T(8,128)(2,1)} %select_select_fusion), calls=%async_computation | async-start | bytes 1048576 | tf_op jit(solution)/shard_map/all_to_all | solution.py:77
  26.1 7.2 %copy-start.17 = (s32[40]{0:T(128)S(1)}, s32[40]{0:T(128)}, u32[]{:S(2)}) copy-start(s32[40]{0:T(128)} %get-tuple-element.51) | copy-start | bytes 484
  26.1 7.2 %copy-start.14 = (pred[40]{0:T(512)(128)(4,1)S(1)}, pred[40]{0:T(512)(128)(4,1)}, u32[]{:S(2)}) copy-start(pred[40]{0:T(512)(128)(4,1)} %iota_compare_fusion.1) | copy-start | bytes 124
  26.1 7.2 %copy-start.19 = (s32[40]{0:T(128)S(1)}, s32[40]{0:T(128)}, u32[]{:S(2)}) copy-start(s32[40]{0:T(128)} %get-tuple-element.53) | copy-start | bytes 484
  26.1 7.2 %copy-start.10 = (s32[40,2]{0,1:T(2,128)S(1)}, s32[40,2]{0,1:T(2,128)}, u32[]{:S(2)}) copy-start(s32[40,2]{0,1:T(2,128)} %param.27) | copy-start | bytes 964
  54.2 3.4 %copy-start.15 = (pred[40]{0:T(512)(128)(4,1)S(1)}, pred[40]{0:T(512)(128)(4,1)}, u32[]{:S(2)}) copy-start(pred[40]{0:T(512)(128)(4,1)} %iota_compare_fusion.1) | copy-start | bytes 124
  57.6 2.5 %copy-start.1 = (bf16[40,128,256]{2,0,1:T(8,128)(2,1)S(1)}, bf16[40,128,256]{2,0,1:T(8,128)(2,1)}, u32[]{:S(2)}) copy-start(bf16[40,128,256]{2,0,1:T(8,128)(2,1)} %copy.23) | copy-start | bytes 7864324
  60.1 5.8 %copy-start.18 = (s32[256]{0:T(256)S(1)}, s32[256]{0:T(256)}, u32[]{:S(2)}) copy-start(s32[256]{0:T(256)} %scatter_custom_fusion.1) | copy-start | bytes 3076
  60.7 19.3 %copy-start.20 = (s32[1,8]{1,0:T(1,128)S(1)}, s32[1,8]{1,0:T(1,128)}, u32[]{:S(2)}) copy-start(s32[1,8]{1,0:T(1,128)} %param.29) | copy-start | bytes 100
  61.6 18.4 %all-to-all-start.1 = ((bf16[8,128,256]{2,1,0:T(8,128)(2,1)}), bf16[8,128,256]{2,1,0:T(8,128)(2,1)S(1)}, u32[]{:S(2)}, u32[]{:S(2)}) async-start(bf16[8,128,256]{2,1,0:T(8,128)(2,1)} %copy.24), calls=%async_computation.1 | async-start | bytes 1048576 | tf_op jit(solution)/shard_map/all_to_all | solution.py:117
  65.8 140.3 %all-reduce.2.cloned.1.call-start = ((), (), s32[]{:S(2)}) async-start(), calls=%async_computation.2 | async-start | bytes 524288 | tf_op jit(solution)/shard_map/psum | solution.py:128
  65.9 14.8 %copy-start.7 = (bf16[256,256]{1,0:T(8,128)(2,1)S(1)}, bf16[256,256]{1,0:T(8,128)(2,1)}, u32[]{:S(2)}) copy-start(bf16[256,256]{1,0:T(8,128)(2,1)} %copy-done.6) | copy-start | bytes 393220
  66.2 14.1 %collective-permute-start.2 = (bf16[256,256]{1,0:T(8,128)(2,1)S(1)}, bf16[256,256]{1,0:T(8,128)(2,1)S(1)}, u32[]{:S(2)}, u32[]{:S(2)}) collective-permute-start(bf16[256,256]{1,0:T(8,128)(2,1)S(1)} %get-tuple-element.46), channel_id=1, source_target_pairs={{0,8},{8,16},{16,24},{24,0},{1,9},{9,17},{17,25},{25,1},{2,10},{10... | collective-permute-start | bytes 393224 | tf_op jit(solution)/shard_map/ppermute | solution.py:16
  66.3 14.1 %collective-permute-start.3 = (bf16[256,256]{1,0:T(8,128)(2,1)S(1)}, bf16[256,256]{1,0:T(8,128)(2,1)S(1)}, u32[]{:S(2)}, u32[]{:S(2)}) collective-permute-start(bf16[256,256]{1,0:T(8,128)(2,1)S(1)} %get-tuple-element.47), channel_id=1, source_target_pairs={{8,0},{16,8},{24,16},{0,24},{9,1},{17,9},{25,17},{1,25},{10,2},{18... | collective-permute-start | bytes 393224 | tf_op jit(solution)/shard_map/ppermute | solution.py:18
  (5 other events, 7.2 us)
Sparse Core Ops, SparseCore 0:
  83.0 123.1 all-reduce.1
where the time goes:
time: 215 us
  waiting for transfers between devices  135 us (63%)
  local copies, waits for them, and re-layouts  26.5 us (12%)
  starting transfers between devices  15.1 us (7%)
  between operations  15.1 us (7%)
  matrix products  12.3 us (6%)
  other arithmetic  10.6 us (5%)
    psum x1, waiting for transfers between devices, on_device(): weight_grad = lax.psum(partial_weight, ('row', 'col')) * nodes_all ** (-0.5)  122 us
    all_to_all x1, waiting for transfers between devices, on_device(): lax.all_to_all(to_owner, 'col', split_axis=0, concat_axis=0, tiled=True)  10.8 us
    all_to_all x1, starting transfers between devices, on_device(): lax.all_to_all(outgoing, 'col', split_axis=0, concat_axis=0, tiled=True)  6.53 us
    dot_general x1, matrix products, on_device(): jnp.einsum('kab,kaf->kbf', bound_tiles, jnp.take(slope_blocks, bound_row_...  4.94 us
    convert_element_type x1, local copies, waits for them, and re-layouts, split_sum(): high_part = terms.astype(jnp.bfloat16)  4.69 us
  transfers between devices with their start and end apart: 7, of which 3 were waited for; matrix products, arithmetic and copies ran while one was open for 9% of the time, Pallas kernels for 0%

commit v1 on v0

--- a/solution.py
+++ b/solution.py
@@ -125,7 +125,9 @@
         x_band, grad_round, (((0,), (0,)), ((), ())), preferred_element_type=jnp.float32
     )
     nodes_all = row_count * lax.axis_size("row") * peers
-    weight_grad = lax.psum(partial_weight, ("row", "col")) * nodes_all ** (-0.5)
+    weight_grad = jnp.sum(lax.all_gather(partial_weight, ("row", "col")), axis=0) * nodes_all ** (
+        -0.5
+    )
     feat_band = lax.dot_general(
         grad_round, weight, (((1,), (1,)), ((), ())), preferred_element_type=jnp.float32
     ).astype(jnp.bfloat16)

time: 215 us -> 169 us (0.79)
  waiting for transfers between devices: 135 us -> 87.9 us
  other arithmetic: 10.6 us -> 13 us
    psum x1 -> x0, waiting for transfers between devices: 122 us -> none  [on_device(): weight_grad = lax.psum(partial_weight, ('row', 'col')) * nodes_all ** (-0.5)]
    all_gather x0 -> x1, waiting for transfers between devices: none -> 70.9 us  [on_device(): lax.all_gather(partial_weight, ('row', 'col'))]
    reduce_sum x0 -> x1, other arithmetic: none -> 3.93 us  [on_device(): jnp.sum(lax.all_gather(partial_weight, ('row', 'col')), axis=0)]
    all_to_all x1, waiting for transfers between devices: 1.76 us -> 4.48 us  [on_device(): lax.all_to_all(outgoing, 'col', split_axis=0, concat_axis=0, tiled=True)]
  transfers between devices with their start and end apart: 7 -> 7, of which waited for: 3 -> 3; matrix products, arithmetic and copies ran while one was open for 9% -> 12% of each run, Pallas kernels for 0% -> 0%
where the time goes in v1:
time: 169 us
  waiting for transfers between devices  87.9 us (52%)
  local copies, waits for them, and re-layouts  25.9 us (15%)
  between operations  15.1 us (9%)
  starting transfers between devices  14.7 us (9%)
  other arithmetic  13 us (8%)
  matrix products  12.3 us (7%)
    all_gather x1, waiting for transfers between devices, on_device(): lax.all_gather(partial_weight, ('row', 'col'))  70.9 us
    all_to_all x1, waiting for transfers between devices, on_device(): lax.all_to_all(to_owner, 'col', split_axis=0, concat_axis=0, tiled=True)  12.5 us
    all_to_all x1, starting transfers between devices, on_device(): lax.all_to_all(outgoing, 'col', split_axis=0, concat_axis=0, tiled=True)  6.53 us
    dot_general x1, matrix products, on_device(): jnp.einsum('kab,kaf->kbf', bound_tiles, jnp.take(slope_blocks, bound_row_...  4.95 us
    convert_element_type x1, local copies, waits for them, and re-layouts, split_sum(): high_part = terms.astype(jnp.bfloat16)  4.74 us
    all_to_all x1, waiting for transfers between devices, on_device(): lax.all_to_all(outgoing, 'col', split_axis=0, concat_axis=0, tiled=True)  4.48 us
    reduce_sum x1, other arithmetic, on_device(): jnp.sum(lax.all_gather(partial_weight, ('row', 'col')), axis=0)  3.93 us
    all_to_all x1, starting transfers between devices, on_device(): lax.all_to_all(to_owner, 'col', split_axis=0, concat_axis=0, tiled=True)  3.77 us
  transfers between devices with their start and end apart: 7, of which 3 were waited for; matrix products, arithmetic and copies ran while one was open for 12% of the time, Pallas kernels for 0%

profile of v1, /device:TPU:0, one launch (start us, length us, event | category | flops | bytes accessed | tf_op | source)
XLA Modules:
  0.0 168.8 jit_solution(10497190896674607106)
XLA Ops:
  8.7 1.9 %gather_fusion.3 = bf16[256,256]{1,0:T(8,128)(2,1)S(1)} fusion(bf16[256,256]{1,0:T(8,128)(2,1)} %param.21, s32[1024]{0:T(1024)S(1)} %pad_clamp_fusion.4), kind=kCustom, calls=%fused_computation.clone | custom fusion | bytes 263168 | tf_op jit(solution)/shard_map/jit(_take)/gather | solution.py:60
  11.4 2.0 %collective-permute-start.1 = (bf16[256,256]{1,0:T(8,128)(2,1)S(1)}, bf16[256,256]{1,0:T(8,128)(2,1)}, u32[]{:S(2)}, u32[]{:S(2)}) collective-permute-start(bf16[256,256]{1,0:T(8,128)(2,1)S(1)} %convolution_convert_fusion.1), channel_id=1, source_target_pairs={{8,0},{16,8},{24,16},{0,24},{9,1},{17,9},{25,17},{1,25},{10,2},{18... | collective-permute-start | bytes 393224 | tf_op jit(solution)/shard_map/ppermute | solution.py:18
  16.3 6.5 %all-to-all-start = ((bf16[8,128,256]{2,1,0:T(8,128)(2,1)}), bf16[8,128,256]{2,1,0:T(8,128)(2,1)S(1)}, u32[]{:S(2)}, u32[]{:S(2)}) async-start(bf16[8,128,256]{2,1,0:T(8,128)(2,1)} %select_select_fusion), calls=%async_computation | async-start | bytes 1048576 | tf_op jit(solution)/shard_map/all_to_all | solution.py:77
  25.5 1.8 %gather_fusion.5 = bf16[256,256]{1,0:T(8,128)(2,1)} fusion(bf16[256,256]{1,0:T(8,128)(2,1)S(1)} %copy-done.2, s32[1024]{0:T(1024)S(1)} %pad_clamp_fusion.4), kind=kCustom, calls=%fused_computation.2.clone | custom fusion | bytes 263168 | tf_op jit(solution)/shard_map/jit(_take)/gather | solution.py:94
  27.4 2.0 %scatter_fusion = bf16[2,128,6,128]{3,1,2,0:T(8,128)(2,1)S(1)} fusion(bf16[2,128,6,128]{3,1,2,0:T(8,128)(2,1)S(1)} %broadcast_in_dim.61, s32[12]{0:T(128)S(1)} %fusion.42, bf16[12,128,128]{2,1,0:T(8,128)(2,1)} %param.24), kind=kCustom, calls=%fused_computation.7 | custom fusion | bytes 1179744 | tf_op jit(solution)/shard_map/scatter | solution.py:66
  29.5 1.1 copy.19
  31.1 1.7 %broadcast_multiply_fusion = bf16[40,2,128,128]{3,0,2,1:T(8,128)(2,1)} fusion(bf16[40,128,128]{2,0,1:T(8,128)(2,1)S(1)} %copy.20, bf16[40,2]{0,1:T(2,128)(2,1)S(1)} %fusion.38), kind=kLoop, calls=%fused_computation.21 | loop fusion | flops 1310720 | bytes 3932320 | tf_op jit(solution)/shard_map/rk,kab->rakb/dot_general | solution.py:84
  32.8 4.5 %all-to-all-done = bf16[8,128,256]{2,1,0:T(8,128)(2,1)S(1)} async-done(((bf16[8,128,256]{2,1,0:T(8,128)(2,1)}), bf16[8,128,256]{2,1,0:T(8,128)(2,1)S(1)}, u32[]{:S(2)}, u32[]{:S(2)}) %all-to-all-start) | async-done | bytes 524320 | tf_op jit(solution)/shard_map/all_to_all | solution.py:77
  38.4 1.4 copy-done.4
  40.8 1.3 multiply_convert_fusion
  42.2 2.4 %gather_fusion.2 = bf16[40,128,256]{2,1,0:T(8,128)(2,1)} fusion(bf16[2,128,256]{2,1,0:T(8,128)(2,1)S(1)} %bitcast.74, s32[1024]{0:T(1024)S(1)} %pad_clamp_fusion), kind=kCustom, calls=%fused_computation.6 | custom fusion | bytes 5243040 | tf_op jit(solution)/shard_map/jit(_take)/gather | solution.py:111
  44.5 5.0 %fusion = (bf16[40,128,256]{1,2,0:T(8,128)(2,1)S(1)}, bf16[40,128,256]{1,2,0:T(8,128)(2,1)}) fusion(bf16[40,128,128]{2,1,0:T(8,128)(2,1)} %param.26, bf16[40,128,256]{2,1,0:T(8,128)(2,1)} %gather_fusion.2, pred[40]{0:T(512)(128)(4,1)S(1)} %copy-done.16), kind=kOutput, calls=%fused_computation.11 | convolution fusion | flops 342097920 | bytes 9175080 | tf_op jit(solution)/shard_map/kab,kaf->kbf/dot_general | solution.py:108
  49.5 4.7 %copy.22 = bf16[40,128,256]{2,0,1:T(8,128)(2,1)} copy(bf16[40,128,256]{1,2,0:T(8,128)(2,1)} %get-tuple-element.45) | data formatting | bytes 5242880 | tf_op jit(solution)/shard_map/convert_element_type | solution.py:26
  54.2 3.4 %copy.23 = bf16[40,128,256]{2,0,1:T(8,128)(2,1)} copy(bf16[40,128,256]{1,2,0:T(8,128)(2,1)S(1)} %get-tuple-element.44) | data formatting | bytes 5242880 | tf_op jit(solution)/shard_map/convert_element_type | solution.py:27
  57.6 2.5 %fusion.28 = f32[8,128,256]{2,0,1:T(8,128)S(1)} fusion(bf16[40,128,256]{2,0,1:T(8,128)(2,1)} %copy.22, s32[40]{0:T(128)S(1)} %get-tuple-element.50, pred[40]{0:T(512)(128)(4,1)S(1)} %copy-done.15), kind=kOutput, calls=%fused_computation.62 | convolution fusion | flops 20972160 | bytes 3670216 | tf_op jit(solution)/shard_map/rk,kaf->raf/dot_general | solution.py:29
  61.6 3.8 %all-to-all-start.1 = ((bf16[8,128,256]{2,1,0:T(8,128)(2,1)}), bf16[8,128,256]{2,1,0:T(8,128)(2,1)S(1)}, u32[]{:S(2)}, u32[]{:S(2)}) async-start(bf16[8,128,256]{2,1,0:T(8,128)(2,1)} %copy.24), calls=%async_computation.1 | async-start | bytes 1048576 | tf_op jit(solution)/shard_map/all_to_all | solution.py:117
  65.8 1.7 %collective-permute-start.3 = (bf16[256,256]{1,0:T(8,128)(2,1)S(1)}, bf16[256,256]{1,0:T(8,128)(2,1)S(1)}, u32[]{:S(2)}, u32[]{:S(2)}) collective-permute-start(bf16[256,256]{1,0:T(8,128)(2,1)S(1)} %get-tuple-element.47), channel_id=1, source_target_pairs={{8,0},{16,8},{24,16},{0,24},{9,1},{17,9},{25,17},{1,25},{10,2},{18... | collective-permute-start | bytes 393224 | tf_op jit(solution)/shard_map/ppermute | solution.py:18
  67.5 12.5 %all-to-all-done.1 = bf16[8,128,256]{2,1,0:T(8,128)(2,1)S(1)} async-done(((bf16[8,128,256]{2,1,0:T(8,128)(2,1)}), bf16[8,128,256]{2,1,0:T(8,128)(2,1)S(1)}, u32[]{:S(2)}, u32[]{:S(2)}) %all-to-all-start.1) | async-done | bytes 524320 | tf_op jit(solution)/shard_map/all_to_all | solution.py:117
  80.6 1.0 fusion.24
  81.7 1.4 scatter_custom_fusion.1
  83.1 1.2 gather_fusion.4
  84.5 1.2 gather_fusion.6
  86.4 70.9 %all-gather.3.cloned.1.call-done = f32[8192,256]{1,0:T(8,128)} async-done(((f32[256,256]{1,0:T(8,128)}), f32[8192,256]{1,0:T(8,128)}) %all-gather.3.cloned.1.call-update) | async-done | bytes 8388624 | tf_op jit(solution)/shard_map/all_gather | solution.py:128
  157.3 3.9 %reduce_sum.9 = f32[256,256]{1,0:T(8,128)S(1)} reduce(f32[32,256,256]{2,1,0:T(8,128)} %bitcast.75, f32[]{:T(128)} %constant.141.clone.1), dimensions={0}, to_apply=%region_2.4 | reduce | flops 2031616 | bytes 8650756 | tf_op jit(solution)/shard_map/reduce_sum | solution.py:128
  (85 shorter events, 13.9 us)
Async XLA Ops:
  7.2 3.4 %copy-start = (bf16[256,256]{1,0:T(8,128)(2,1)S(1)}, bf16[256,256]{1,0:T(8,128)(2,1)}, u32[]{:S(2)}) copy-start(bf16[256,256]{1,0:T(8,128)(2,1)} %param.22) | copy-start | bytes 393220
  7.2 15.6 %copy-start.9 = (s32[40,2]{0,1:T(2,128)S(1)}, s32[40,2]{0,1:T(2,128)}, u32[]{:S(2)}) copy-start(s32[40,2]{0,1:T(2,128)} %param.27) | copy-start | bytes 964
  7.2 16.8 %copy-start.20 = (s32[12,2]{0,1:T(2,128)S(1)}, s32[12,2]{0,1:T(2,128)}, u32[]{:S(2)}) copy-start(s32[12,2]{0,1:T(2,128)} %param.25) | copy-start | bytes 292
  7.2 17.4 %copy-start.3 = (bf16[40,128,128]{2,1,0:T(8,128)(2,1)S(1)}, bf16[40,128,128]{2,1,0:T(8,128)(2,1)}, u32[]{:S(2)}) copy-start(bf16[40,128,128]{2,1,0:T(8,128)(2,1)} %param.26) | copy-start | bytes 3932164
  8.7 5.3 %copy-start.12 = (pred[256]{0:T(512)(128)(4,1)}, pred[256]{0:T(512)(128)(4,1)S(1)}, u32[]{:S(2)}) copy-start(pred[256]{0:T(512)(128)(4,1)S(1)} %compare_and_fusion.1) | copy-start | bytes 772
  10.6 4.1 %copy-start.6 = (bf16[256,256]{1,0:T(8,128)(2,1)}, bf16[256,256]{1,0:T(8,128)(2,1)S(1)}, u32[]{:S(2)}) copy-start(bf16[256,256]{1,0:T(8,128)(2,1)S(1)} %gather_fusion.3) | copy-start | bytes 393220
  10.9 29.8 %collective-permute-start = (bf16[256,256]{1,0:T(8,128)(2,1)S(1)}, bf16[256,256]{1,0:T(8,128)(2,1)}, u32[]{:S(2)}, u32[]{:S(2)}) collective-permute-start(bf16[256,256]{1,0:T(8,128)(2,1)S(1)} %convolution_convert_fusion.1), channel_id=1, source_target_pairs={{0,8},{8,16},{16,24},{24,0},{1,9},{9,17},{17,25},{25,1},{2,10},{10... | collective-permute-start | bytes 393224 | tf_op jit(solution)/shard_map/ppermute | solution.py:16
  11.4 29.3 %collective-permute-start.1 = (bf16[256,256]{1,0:T(8,128)(2,1)S(1)}, bf16[256,256]{1,0:T(8,128)(2,1)}, u32[]{:S(2)}, u32[]{:S(2)}) collective-permute-start(bf16[256,256]{1,0:T(8,128)(2,1)S(1)} %convolution_convert_fusion.1), channel_id=1, source_target_pairs={{8,0},{16,8},{24,16},{0,24},{9,1},{17,9},{25,17},{1,25},{10,2},{18... | collective-permute-start | bytes 393224 | tf_op jit(solution)/shard_map/ppermute | solution.py:18
  15.3 10.2 %copy-start.2 = (bf16[256,256]{1,0:T(8,128)(2,1)S(1)}, bf16[256,256]{1,0:T(8,128)(2,1)}, u32[]{:S(2)}) copy-start(bf16[256,256]{1,0:T(8,128)(2,1)} %param.23) | copy-start | bytes 393220
  16.3 21.1 %all-to-all-start = ((bf16[8,128,256]{2,1,0:T(8,128)(2,1)}), bf16[8,128,256]{2,1,0:T(8,128)(2,1)S(1)}, u32[]{:S(2)}, u32[]{:S(2)}) async-start(bf16[8,128,256]{2,1,0:T(8,128)(2,1)} %select_select_fusion), calls=%async_computation | async-start | bytes 1048576 | tf_op jit(solution)/shard_map/all_to_all | solution.py:77
  25.5 5.1 %copy-start.17 = (s32[40]{0:T(128)S(1)}, s32[40]{0:T(128)}, u32[]{:S(2)}) copy-start(s32[40]{0:T(128)} %get-tuple-element.51) | copy-start | bytes 484
  25.5 5.1 %copy-start.14 = (pred[40]{0:T(512)(128)(4,1)S(1)}, pred[40]{0:T(512)(128)(4,1)}, u32[]{:S(2)}) copy-start(pred[40]{0:T(512)(128)(4,1)} %iota_compare_fusion.1) | copy-start | bytes 124
  25.5 5.1 %copy-start.18 = (s32[40]{0:T(128)S(1)}, s32[40]{0:T(128)}, u32[]{:S(2)}) copy-start(s32[40]{0:T(128)} %get-tuple-element.53) | copy-start | bytes 484
  25.5 5.1 %copy-start.10 = (s32[40,2]{0,1:T(2,128)S(1)}, s32[40,2]{0,1:T(2,128)}, u32[]{:S(2)}) copy-start(s32[40,2]{0,1:T(2,128)} %param.27) | copy-start | bytes 964
  42.2 2.4 %copy-start.16 = (pred[40]{0:T(512)(128)(4,1)S(1)}, pred[40]{0:T(512)(128)(4,1)}, u32[]{:S(2)}) copy-start(pred[40]{0:T(512)(128)(4,1)} %get-tuple-element.54) | copy-start | bytes 124
  54.2 3.4 %copy-start.15 = (pred[40]{0:T(512)(128)(4,1)S(1)}, pred[40]{0:T(512)(128)(4,1)}, u32[]{:S(2)}) copy-start(pred[40]{0:T(512)(128)(4,1)} %iota_compare_fusion.1) | copy-start | bytes 124
  57.6 2.5 %copy-start.1 = (bf16[40,128,256]{2,0,1:T(8,128)(2,1)S(1)}, bf16[40,128,256]{2,0,1:T(8,128)(2,1)}, u32[]{:S(2)}) copy-start(bf16[40,128,256]{2,0,1:T(8,128)(2,1)} %copy.23) | copy-start | bytes 7864324
  60.7 19.3 %copy-start.19 = (s32[1,8]{1,0:T(1,128)S(1)}, s32[1,8]{1,0:T(1,128)}, u32[]{:S(2)}) copy-start(s32[1,8]{1,0:T(1,128)} %param.29) | copy-start | bytes 100
  61.6 19.0 %copy-start.7 = (bf16[256,256]{1,0:T(8,128)(2,1)S(1)}, bf16[256,256]{1,0:T(8,128)(2,1)}, u32[]{:S(2)}) copy-start(bf16[256,256]{1,0:T(8,128)(2,1)} %copy-done.6) | copy-start | bytes 393220
  61.6 18.4 %all-to-all-start.1 = ((bf16[8,128,256]{2,1,0:T(8,128)(2,1)}), bf16[8,128,256]{2,1,0:T(8,128)(2,1)S(1)}, u32[]{:S(2)}, u32[]{:S(2)}) async-start(bf16[8,128,256]{2,1,0:T(8,128)(2,1)} %copy.24), calls=%async_computation.1 | async-start | bytes 1048576 | tf_op jit(solution)/shard_map/all_to_all | solution.py:117
  65.4 16.2 %copy-start.11 = (s32[1,256]{1,0:T(1,128)S(1)}, s32[1,256]{1,0:T(1,128)}, u32[]{:S(2)}) copy-start(s32[1,256]{1,0:T(1,128)} %param.30) | copy-start | bytes 3076
  65.4 91.9 %all-gather.3.cloned.1.call-start = ((), (), s32[]{:S(2)}) async-start(), calls=%async_computation.2 | async-start | bytes 8650752 | tf_op jit(solution)/shard_map/all_gather | solution.py:128
  65.7 14.8 %collective-permute-start.2 = (bf16[256,256]{1,0:T(8,128)(2,1)S(1)}, bf16[256,256]{1,0:T(8,128)(2,1)S(1)}, u32[]{:S(2)}, u32[]{:S(2)}) collective-permute-start(bf16[256,256]{1,0:T(8,128)(2,1)S(1)} %get-tuple-element.46), channel_id=1, source_target_pairs={{0,8},{8,16},{16,24},{24,0},{1,9},{9,17},{17,25},{25,1},{2,10},{10... | collective-permute-start | bytes 393224 | tf_op jit(solution)/shard_map/ppermute | solution.py:16
  65.8 14.7 %collective-permute-start.3 = (bf16[256,256]{1,0:T(8,128)(2,1)S(1)}, bf16[256,256]{1,0:T(8,128)(2,1)S(1)}, u32[]{:S(2)}, u32[]{:S(2)}) collective-permute-start(bf16[256,256]{1,0:T(8,128)(2,1)S(1)} %get-tuple-element.47), channel_id=1, source_target_pairs={{8,0},{16,8},{24,16},{0,24},{9,1},{17,9},{25,17},{1,25},{10,2},{18... | collective-permute-start | bytes 393224 | tf_op jit(solution)/shard_map/ppermute | solution.py:18
  (4 other events, 4.8 us)
Sparse Core Ops, SparseCore 0:
  81.7 75.5 all-gather.2
